TPU v7x, 512 devices: a whole 4x4x16 slice. The times are simulated.
512 devices in a mesh: tm: 16 (over z_hi, y), space: 32 (over z_lo, x, core).
Axes of the slice: x: 4, y: 4, z: 16 (z_hi: 4, z_lo: 4; z = z_hi * 4 + z_lo), core: 2. Of those that a mesh axis runs over, the one named last changes fastest.
Arguments:
- queries: bfloat16 [128, 2048, 256], P('tm', 'space'), as said below
- keys: bfloat16 [128, 2048, 256], P('tm', 'space'), as said below
- label_values: bfloat16 [128, 2048, 64], P('tm', 'space'), may hold values from -6 to 6
- class_ids: int32 [128, 2048], P(None, 'space'), may hold values from 0 to 63
- valid_pixels: int32 [128], replicated, may hold values from 1024 to 2048
- keyframe_index: int32 [2, 2], replicated, may hold values from 0 to 127, as said below
Outputs:
- readout: bfloat16 [128, 2048, 64], P('tm', 'space')
- confidence: float32 [2, 2, 2048], P(None, None, 'space')
Inputs may be any that keep to these rules, and one draw needn't show every extreme that they name: `queries`: queries and keys are real-valued embeddings. `keys`: Real-valued embeddings. `keyframe_index`: all 4 entries are different frames.
All inputs are finite; a program needn't handle non-finite values.
Results may differ from a plain program's by a relative error of at most 0.0053.
Values may be sent and summed in bfloat16 or wider, within the bound.
No kernel may reach another device: no remote copies, remote signals or barrier semaphores. Data moves between devices by JAX's collectives and lax.ppermute only.
A program may use at most 192 MiB of HBM per device.

v0:
```python
import math
import jax
import jax.numpy as jnp
from jax import lax
from jax.sharding import PartitionSpec as P


def from_root(value, axis, root):
    mine = lax.axis_index(axis) == root
    return lax.psum(jnp.where(mine, value, jnp.zeros_like(value)), axis)


def body(queries, keys, label_values, class_ids, valid_pixels, keyframe_index):
    fr_dev, pix_dev, width = queries.shape
    channels = label_values.shape[2]
    total_steps, keyframes = keyframe_index.shape
    pix_all = pix_dev * lax.axis_size("space")
    mem_width = keyframes * pix_all
    time_pos = lax.axis_index("tm")
    space_pos = lax.axis_index("space")
    rows = fr_dev * pix_dev
    block_rows = 512
    blocks = rows // block_rows
    frame_valid = lax.dynamic_slice_in_dim(valid_pixels, time_pos * fr_dev, fr_dev)
    pixel_ids = space_pos * pix_dev + jnp.arange(pix_dev, dtype=jnp.int32)
    row_valid = (pixel_ids[None, :] < frame_valid[:, None]).reshape(blocks, block_rows)
    query_blocks = queries.reshape(blocks, block_rows, width)
    scale = 3.0 / math.sqrt(width)
    class_range = jnp.arange(channels, dtype=jnp.int32)
    current = label_values
    confidences = []
    readout = label_values
    for step in range(total_steps):
        chosen = keyframe_index[step]
        owners = chosen // fr_dev
        slots = chosen % fr_dev
        local_keys = jnp.take(keys, slots, axis=0)
        local_values = jnp.take(current, slots, axis=0)
        joined = jnp.concatenate([local_keys, local_values], axis=2)
        fetched = []
        for number in range(keyframes):
            fetched.append(from_root(joined[number], "tm", owners[number]))
        fetched = jnp.stack(fetched)
        part_keys = fetched[:, :, :width]
        part_values = fetched[:, :, width:]
        part_ids = jnp.take(class_ids, chosen, axis=0).astype(jnp.bfloat16)
        mem_keys, mem_values, mem_ids = (
            lax.all_gather(part_keys, "space", axis=1, tiled=True),
            lax.all_gather(part_values, "space", axis=1, tiled=True),
            lax.all_gather(part_ids, "space", axis=1, tiled=True),
        )
        mem_keys = mem_keys.reshape(mem_width, width)
        mem_values = mem_values.reshape(mem_width, channels)
        mem_ids = mem_ids.reshape(mem_width).astype(jnp.int32)
        key_valid = (
            jnp.arange(pix_all, dtype=jnp.int32)[None, :] < jnp.take(valid_pixels, chosen)[:, None]
        ).reshape(mem_width)
        class_match = mem_ids[None, :] == class_range[:, None]
        onehot_t = class_match.astype(jnp.bfloat16)

        def score_block(query_rows):
            raw = lax.dot_general(
                query_rows, mem_keys, (((1,), (1,)), ((), ())), preferred_element_type=jnp.float32
            )
            return raw * scale

        def forward(scores, valid_rows):
            masked = jnp.where(key_valid[None, :], scores, -1e30)
            row_max = jnp.max(masked, axis=1, keepdims=True)
            weights = jnp.where(key_valid[None, :], jnp.exp(scores - row_max), 0.0)
            total = jnp.sum(weights, axis=1, keepdims=True)
            mixed = (
                jnp.dot(
                    weights.astype(jnp.bfloat16), mem_values, preferred_element_type=jnp.float32
                )
                / total
            )
            return jnp.where(valid_rows[:, None], mixed, 0.0).astype(jnp.bfloat16)

        lowest = jnp.full((mem_width,), -1e30, jnp.float32)
        zeros_col = jnp.zeros((mem_width,), jnp.float32)

        def first_pass(col_max, inputs):
            query_rows, valid_rows = inputs
            scores = score_block(query_rows)
            block_out = forward(scores, valid_rows)
            local_max = jnp.max(jnp.where(valid_rows[:, None], scores, -1e30), axis=0)
            return (jnp.maximum(col_max, local_max), block_out)

        col_max, out_blocks = lax.scan(first_pass, lowest, (query_blocks, row_valid))
        col_max = lax.pmax(col_max, ("tm", "space"))

        def second_pass(carry, inputs):
            query_rows, valid_rows, block_out = inputs
            scores = score_block(query_rows)
            expo = jnp.where(valid_rows[:, None], jnp.exp(scores - col_max[None, :]), 0.0)
            picked = jnp.dot(block_out, onehot_t, preferred_element_type=jnp.float32)
            return (
                (carry[0] + jnp.sum(expo, axis=0), carry[1] + jnp.sum(expo * picked, axis=0)),
                None,
            )

        (col_total, col_num), unused = lax.scan(
            second_pass, (zeros_col, zeros_col), (query_blocks, row_valid, out_blocks)
        )
        col_total, col_num = lax.psum((col_total, col_num), ("tm", "space"))
        readout = out_blocks.reshape(fr_dev, pix_dev, channels)
        hits = (class_match & key_valid[None, :]).astype(jnp.int32)
        counts = jnp.sum(hits, axis=1)
        all_count = jnp.sum(counts)
        own = jnp.sum(jnp.where(class_match, counts[:, None], 0), axis=0)
        own_safe = jnp.where(key_valid, own, 1)
        factor = jnp.sqrt(all_count.astype(jnp.float32) / (channels * own_safe.astype(jnp.float32)))
        conf_full = jnp.where(key_valid, col_num / col_total * factor, 0.0).reshape(
            keyframes, pix_all
        )
        confidences.append(lax.dynamic_slice_in_dim(conf_full, space_pos * pix_dev, pix_dev, 1))
        current = readout
    return (readout, jnp.stack(confidences))


def solution(mesh):
    placed = (
        P("tm", "space", None),
        P("tm", "space", None),
        P("tm", "space", None),
        P(None, "space"),
        P(),
        P(),
    )
    return jax.shard_map(
        body,
        mesh=mesh,
        in_specs=placed,
        out_specs=(P("tm", "space", None), P(None, None, "space")),
        check_vma=False,
    )
```

profile of v0, /device:TPU:1, one launch (start us, length us, event | category | flops | bytes accessed | tf_op | source)
XLA Modules:
  0.0 1291.4 jit_solution(1095203512651782425)
XLA Ops:
  7.2 0.8 and_select_fusion.1
  8.0 1.5 gather_fusion.3
  9.5 1.5 gather_fusion.4
  13.9 188.7 %all-reduce.11.cloned.1.call-done = (bf16[1,64,320]{2,1,0:T(8,128)(2,1)}, bf16[1,64,320]{2,1,0:T(8,128)(2,1)}) async-done(((bf16[1,64,320]{2,1,0:T(8,128)(2,1)}, bf16[1,64,320]{2,1,0:T(8,128)(2,1)}), (bf16[1,64,320]{2,1,0:T(8,128)(2,1)}, bf16[1,64,320]{2,1,0:T(8,128)(2,1)})) %all-reduce.11.cloned.1.call-update) | async-done | bytes 81936 | tf_op jit(solution)/shard_map/psum | solution.py:10
  202.6 0.8 constant_dynamic-update-slice_fusion.1
  203.4 0.8 constant_dynamic-update-slice_fusion
  205.9 0.8 compare_and_fusion.3
  206.6 1.3 gather_fusion.2
  207.9 1.3 gather_fusion
  209.4 1.5 gather_fusion.1
  212.3 56.8 %all_gather.19 = bf16[2,2048,64]{2,1,0:T(8,128)(2,1)S(1)} all-gather(bf16[2,64,64]{2,1,0:T(8,128)(2,1)S(1)} %slice.75), channel_id=1, replica_groups=mesh['tm'=16,'space'=32] {'space'}, dimensions={1}, use_global_device_ids=true | all-gather | bytes 540672 | tf_op jit(solution)/shard_map/all_gather | solution.py:49
  269.1 13.7 %all-gather.5.cloned.1.call-done = bf16[2,2048,256]{2,1,0:T(8,128)(2,1)} async-done(((bf16[2,64,256]{2,1,0:T(8,128)(2,1)}), bf16[2,2048,256]{2,1,0:T(8,128)(2,1)}) %all-gather.5.cloned.1.call-update) | async-done | bytes 2097168 | tf_op jit(solution)/shard_map/all_gather | solution.py:48
  282.8 6.0 select_reduce_fusion.1
  288.9 104.7 %pmax.14 = f32[4096]{0:T(1024)S(1)} all-reduce(f32[4096]{0:T(1024)S(1)} %broadcast_maximum_fusion.1), channel_id=1, replica_groups=mesh['tm'=16,'space'=32] {'tm','space'}, use_global_device_ids=true, to_apply=%region_9.13 | all-reduce | flops 4096 | bytes 32768 | tf_op jit(solution)/shard_map/pmax | solution.py:91
  393.5 7.0 fusion.6
  400.6 1.5 fusion.20
  403.6 176.6 %all-reduce.9.cloned.1.call-done = (bf16[1,64,320]{2,1,0:T(8,128)(2,1)}, bf16[1,64,320]{2,1,0:T(8,128)(2,1)}) async-done(((bf16[1,64,320]{2,1,0:T(8,128)(2,1)}, bf16[1,64,320]{2,1,0:T(8,128)(2,1)}), (bf16[1,64,320]{2,1,0:T(8,128)(2,1)}, bf16[1,64,320]{2,1,0:T(8,128)(2,1)})) %all-reduce.9.cloned.1.call-update) | async-done | bytes 81936 | tf_op jit(solution)/shard_map/psum | solution.py:10
  580.2 0.8 constant_dynamic-update-slice_fusion.3
  581.0 0.8 constant_dynamic-update-slice_fusion.2
  583.8 53.1 %all-gather = bf16[32,64,2]{1,2,0:T(2,128)(2,1)S(1)} all-gather(bf16[1,64,2]{1,2,0:T(2,128)(2,1)S(1)} %fusion.42), channel_id=1, replica_groups=mesh['tm'=16,'space'=32] {'space'}, dimensions={0}, use_global_device_ids=true | all-gather | bytes 8448 | tf_op jit(solution)/shard_map/all_gather | solution.py:50
  637.2 37.6 %all-gather.1 = bf16[32,64,2]{1,2,0:T(2,128)(2,1)S(1)} all-gather(bf16[1,64,2]{1,2,0:T(2,128)(2,1)S(1)} %fusion.43), channel_id=1, replica_groups=mesh['tm'=16,'space'=32] {'space'}, dimensions={0}, use_global_device_ids=true | all-gather | bytes 8448 | tf_op jit(solution)/shard_map/all_gather | solution.py:50
  674.9 1.1 convert_reduce_fusion.3
  676.0 1.0 convert_reduce_fusion.1
  677.2 5.3 fusion.1
  682.5 42.2 %all_gather.21 = bf16[2,2048,64]{2,1,0:T(8,128)(2,1)S(1)} all-gather(bf16[2,64,64]{2,1,0:T(8,128)(2,1)S(1)} %slice.79), channel_id=1, replica_groups=mesh['tm'=16,'space'=32] {'space'}, dimensions={1}, use_global_device_ids=true | all-gather | bytes 540672 | tf_op jit(solution)/shard_map/all_gather | solution.py:49
  724.7 6.0 select_reduce_fusion
  730.7 101.4 %pmax.15 = f32[4096]{0:T(1024)S(1)} all-reduce(f32[4096]{0:T(1024)S(1)} %broadcast_maximum_fusion), channel_id=1, replica_groups=mesh['tm'=16,'space'=32] {'tm','space'}, use_global_device_ids=true, to_apply=%region_18.23 | all-reduce | flops 4096 | bytes 32768 | tf_op jit(solution)/shard_map/pmax | solution.py:91
  832.1 7.0 fusion.7
  839.1 1.5 fusion.29
  840.6 3.2 fusion
  846.2 436.3 %all-reduce.7.cloned.1.call-done = (f32[4096]{0:T(1024)}, f32[4096]{0:T(1024)}, f32[4096]{0:T(1024)}, f32[4096]{0:T(1024)}) async-done(((f32[4096]{0:T(1024)}, f32[4096]{0:T(1024)}, f32[4096]{0:T(1024)}, f32[4096]{0:T(1024)}), (f32[4096]{0:T(1024)}, f32[4096]{0:T(1024)}, f32[4096]{0:T(1024)}, f32[4096]{0:T(1024)})) %all-reduce.7.cloned.1.call-update) | async-done | bytes 65552 | tf_op jit(solution)/shard_map/psum | solution.py:106
  1283.3 0.8 multiply_select_fusion
  (68 shorter events, 10.0 us)
Async XLA Ops:
  7.2 275.7 %copy-start = (bf16[8,64,256]{2,1,0:T(8,128)(2,1)S(1)}, bf16[8,64,256]{2,1,0:T(8,128)(2,1)}, u32[]{:S(2)}) copy-start(bf16[8,64,256]{2,1,0:T(8,128)(2,1)} %param.14) | copy-start | bytes 786436
  7.2 195.5 %all-reduce.11.cloned.1.call-start = ((), (), s32[]{:S(2)}) async-start(), calls=%async_computation.4 | async-start | bytes 196608 | tf_op jit(solution)/shard_map/psum | solution.py:10
  13.9 269.0 %all-gather.5.cloned.1.call-start = ((), (), s32[]{:S(2)}) async-start(), calls=%async_computation | async-start | bytes 2162688 | tf_op jit(solution)/shard_map/all_gather | solution.py:48
  204.9 375.2 %all-reduce.9.cloned.1.call-start = ((), (), s32[]{:S(2)}) async-start(), calls=%async_computation.3 | async-start | bytes 196608 | tf_op jit(solution)/shard_map/psum | solution.py:10
  393.5 7.0 copy-start.1
  393.5 188.9 %copy-start.3 = (s32[128,64]{0,1:T(8,128)S(1)}, s32[128,64]{0,1:T(8,128)}, u32[]{:S(2)}) copy-start(s32[128,64]{0,1:T(8,128)} %param.17) | copy-start | bytes 98308
  403.5 321.1 %all-gather.7.cloned.1.call-start = ((), (), s32[]{:S(2)}) async-start(), calls=%async_computation.1 | async-start | bytes 2162688 | tf_op jit(solution)/shard_map/all_gather | solution.py:48
  582.4 700.1 %all-reduce.7.cloned.1.call-start = ((), (), s32[]{:S(2)}) async-start(), calls=%async_computation.2 | async-start | bytes 131072 | tf_op jit(solution)/shard_map/psum | solution.py:106
  832.1 7.0 copy-start.2
Sparse Core Ops, SparseCore 0:
  14.0 188.6 all-reduce.10
  205.6 77.1 all-gather.4
  403.7 176.4 all-reduce.8
  582.7 77.0 all-gather.6
  844.0 438.5 all-reduce.6
where the time goes:
time: 1290 us
  waiting for transfers between devices  815 us (63%)
  blocking collectives  396 us (31%)
  matrix products  23.6 us (2%)
  other arithmetic  22.3 us (2%)
  between operations  17.9 us (1%)
  local copies, waits for them, and re-layouts  16.1 us (1%)
    psum x1, waiting for transfers between devices, body(): col_total, col_num = lax.psum((col_total, col_num), ('tm', 'space'))  436 us
    psum x2, waiting for transfers between devices, from_root(): return lax.psum(jnp.where(mine, value, jnp.zeros_like(value)), axis)  365 us
    pmax x2, blocking collectives, body(): col_max = lax.pmax(col_max, ('tm', 'space'))  206 us
    all_gather x2, blocking collectives, body(): lax.all_gather(part_values, 'space', axis=1, tiled=True)  99 us
    all_gather x2, blocking collectives, body(): lax.all_gather(part_ids, 'space', axis=1, tiled=True)  90.7 us
  transfers between devices with their start and end apart: 5, of which 4 were waited for; matrix products, arithmetic and copies ran while one was open for 1% of the time, Pallas kernels for 0%

commit v1 on v0

--- a/solution.py
+++ b/solution.py
@@ -3,11 +3,16 @@
 import jax.numpy as jnp
 from jax import lax
 from jax.sharding import PartitionSpec as P
+from jax.lax import all_gather
 
 
 def from_root(value, axis, root):
     mine = lax.axis_index(axis) == root
-    return lax.psum(jnp.where(mine, value, jnp.zeros_like(value)), axis)
+
+    def cycles_refer(page, across):
+        return all_gather(page, across).sum(axis=0)
+
+    return cycles_refer(jnp.where(mine, value, jnp.zeros_like(value)), axis)
 
 
 def body(queries, keys, label_values, class_ids, valid_pixels, keyframe_index):

time: 1290 us -> 1130 us (0.88)
  waiting for transfers between devices: 815 us -> 440 us
  blocking collectives: 396 us -> 617 us
    psum x2 -> x0, waiting for transfers between devices: 365 us -> none  [from_root(): return lax.psum(jnp.where(mine, value, jnp.zeros_like(value)), axis)]
    all_gather x0 -> x4, blocking collectives: none -> 216 us  [cycles_refer(): return all_gather(page, across).sum(axis=0)]
  transfers between devices with their start and end apart: 5 -> 3, of which waited for: 4 -> 2; matrix products, arithmetic and copies ran while one was open for 1% -> 1% of each run, Pallas kernels for 0% -> 0%
where the time goes in v1:
time: 1130 us
  blocking collectives  617 us (55%)
  waiting for transfers between devices  440 us (39%)
  matrix products  23.6 us (2%)
  other arithmetic  22.8 us (2%)
  between operations  17.8 us (2%)
  local copies, waits for them, and re-layouts  11.6 us (1%)
    psum x1, waiting for transfers between devices, body(): col_total, col_num = lax.psum((col_total, col_num), ('tm', 'space'))  436 us
    all_gather x4, blocking collectives, cycles_refer(): return all_gather(page, across).sum(axis=0)  216 us
    pmax x2, blocking collectives, body(): col_max = lax.pmax(col_max, ('tm', 'space'))  204 us
    all_gather x2, blocking collectives, body(): lax.all_gather(part_values, 'space', axis=1, tiled=True)  108 us
    all_gather x2, blocking collectives, body(): lax.all_gather(part_ids, 'space', axis=1, tiled=True)  88.3 us
  transfers between devices with their start and end apart: 3, of which 2 were waited for; matrix products, arithmetic and copies ran while one was open for 1% of the time, Pallas kernels for 0%

profile of v1, /device:TPU:1, one launch (start us, length us, event | category | flops | bytes accessed | tf_op | source)
XLA Modules:
  0.0 1133.1 jit_solution(5651233344326770821)
XLA Ops:
  7.2 0.8 and_select_fusion.3
  8.0 1.5 gather_fusion.3
  9.5 1.5 gather_fusion.4
  13.1 62.1 %all_gather.34 = bf16[16,64,320]{2,1,0:T(8,128)(2,1)S(1)} all-gather(bf16[1,64,320]{2,1,0:T(8,128)(2,1)S(1)} %get-tuple-element.148), channel_id=1, replica_groups=mesh['tm'=16,'space'=32] {'tm'}, dimensions={0}, use_global_device_ids=true | all-gather | bytes 696320 | tf_op jit(solution)/shard_map/all_gather | solution.py:13
  75.2 46.3 %all_gather.35 = bf16[16,64,320]{2,1,0:T(8,128)(2,1)S(1)} all-gather(bf16[1,64,320]{2,1,0:T(8,128)(2,1)S(1)} %get-tuple-element.149), channel_id=1, replica_groups=mesh['tm'=16,'space'=32] {'tm'}, dimensions={0}, use_global_device_ids=true | all-gather | bytes 696320 | tf_op jit(solution)/shard_map/all_gather | solution.py:13
  123.4 0.8 compare_and_fusion.3
  124.2 1.3 gather_fusion.2
  125.5 1.3 gather_fusion
  126.9 1.5 gather_fusion.1
  129.8 67.0 %all_gather.37 = bf16[2,2048,64]{2,1,0:T(8,128)(2,1)S(1)} all-gather(bf16[2,64,64]{2,1,0:T(8,128)(2,1)S(1)} %pad_maximum_fusion.3), channel_id=1, replica_groups=mesh['tm'=16,'space'=32] {'space'}, dimensions={1}, use_global_device_ids=true | all-gather | bytes 540672 | tf_op jit(solution)/shard_map/all_gather | solution.py:54
  196.9 4.7 all-gather.5.cloned.1.call-done
  201.6 6.0 select_reduce_fusion.1
  207.6 104.2 %pmax.14 = f32[4096]{0:T(1024)S(1)} all-reduce(f32[4096]{0:T(1024)S(1)} %broadcast_maximum_fusion.1), channel_id=1, replica_groups=mesh['tm'=16,'space'=32] {'tm','space'}, use_global_device_ids=true, to_apply=%region_9.13 | all-reduce | flops 4096 | bytes 32768 | tf_op jit(solution)/shard_map/pmax | solution.py:96
  311.9 7.0 fusion.6
  318.9 1.5 fusion.20
  321.2 57.3 %all_gather.38 = bf16[16,64,320]{2,1,0:T(8,128)(2,1)S(1)} all-gather(bf16[1,64,320]{2,1,0:T(8,128)(2,1)S(1)} %get-tuple-element.146), channel_id=1, replica_groups=mesh['tm'=16,'space'=32] {'tm'}, dimensions={0}, use_global_device_ids=true | all-gather | bytes 696320 | tf_op jit(solution)/shard_map/all_gather | solution.py:13
  378.7 50.3 %all_gather.39 = bf16[16,64,320]{2,1,0:T(8,128)(2,1)S(1)} all-gather(bf16[1,64,320]{2,1,0:T(8,128)(2,1)S(1)} %get-tuple-element.147), channel_id=1, replica_groups=mesh['tm'=16,'space'=32] {'tm'}, dimensions={0}, use_global_device_ids=true | all-gather | bytes 696320 | tf_op jit(solution)/shard_map/all_gather | solution.py:13
  431.1 49.0 %all-gather = bf16[32,64,2]{1,2,0:T(2,128)(2,1)S(1)} all-gather(bf16[1,64,2]{1,2,0:T(2,128)(2,1)S(1)} %fusion.44), channel_id=1, replica_groups=mesh['tm'=16,'space'=32] {'space'}, dimensions={0}, use_global_device_ids=true | all-gather | bytes 8448 | tf_op jit(solution)/shard_map/all_gather | solution.py:55
  480.4 39.3 %all-gather.1 = bf16[32,64,2]{1,2,0:T(2,128)(2,1)S(1)} all-gather(bf16[1,64,2]{1,2,0:T(2,128)(2,1)S(1)} %fusion.45), channel_id=1, replica_groups=mesh['tm'=16,'space'=32] {'space'}, dimensions={0}, use_global_device_ids=true | all-gather | bytes 8448 | tf_op jit(solution)/shard_map/all_gather | solution.py:55
  519.8 1.1 convert_reduce_fusion.3
  520.9 1.0 convert_reduce_fusion.1
  522.1 40.9 %all_gather.41 = bf16[2,2048,64]{2,1,0:T(8,128)(2,1)S(1)} all-gather(bf16[2,64,64]{2,1,0:T(8,128)(2,1)S(1)} %pad_maximum_fusion.2), channel_id=1, replica_groups=mesh['tm'=16,'space'=32] {'space'}, dimensions={1}, use_global_device_ids=true | all-gather | bytes 540672 | tf_op jit(solution)/shard_map/all_gather | solution.py:54
  563.1 5.3 fusion.1
  568.3 6.0 select_reduce_fusion
  574.4 100.0 %pmax.15 = f32[4096]{0:T(1024)S(1)} all-reduce(f32[4096]{0:T(1024)S(1)} %broadcast_maximum_fusion), channel_id=1, replica_groups=mesh['tm'=16,'space'=32] {'tm','space'}, use_global_device_ids=true, to_apply=%region_18.23 | all-reduce | flops 4096 | bytes 32768 | tf_op jit(solution)/shard_map/pmax | solution.py:96
  674.4 7.0 fusion.7
  681.5 1.5 fusion.29
  683.0 3.2 fusion
  687.8 0.8 copy.36
  688.5 435.7 %all-reduce.3.cloned.1.call-done = (f32[4096]{0:T(1024)}, f32[4096]{0:T(1024)}, f32[4096]{0:T(1024)}, f32[4096]{0:T(1024)}) async-done(((f32[4096]{0:T(1024)}, f32[4096]{0:T(1024)}, f32[4096]{0:T(1024)}, f32[4096]{0:T(1024)}), (f32[4096]{0:T(1024)}, f32[4096]{0:T(1024)}, f32[4096]{0:T(1024)}, f32[4096]{0:T(1024)})) %all-reduce.3.cloned.1.call-update) | async-done | bytes 65552 | tf_op jit(solution)/shard_map/psum | solution.py:111
  1124.3 0.8 multiply_select_fusion.1
  1125.0 0.8 multiply_select_fusion
  (66 shorter events, 7.7 us)
Async XLA Ops:
  7.2 194.4 %copy-start = (bf16[8,64,256]{2,1,0:T(8,128)(2,1)S(1)}, bf16[8,64,256]{2,1,0:T(8,128)(2,1)}, u32[]{:S(2)}) copy-start(bf16[8,64,256]{2,1,0:T(8,128)(2,1)} %param.14) | copy-start | bytes 786436
  7.2 194.4 %all-gather.5.cloned.1.call-start = ((), (), s32[]{:S(2)}) async-start(), calls=%async_computation | async-start | bytes 2162688 | tf_op jit(solution)/shard_map/all_gather | solution.py:53
  122.4 445.9 %all-gather.7.cloned.1.call-start = ((), (), s32[]{:S(2)}) async-start(), calls=%async_computation.1 | async-start | bytes 2162688 | tf_op jit(solution)/shard_map/all_gather | solution.py:53
  311.9 7.0 copy-start.1
  318.9 110.9 %copy-start.3 = (s32[128,64]{0,1:T(8,128)S(1)}, s32[128,64]{0,1:T(8,128)}, u32[]{:S(2)}) copy-start(s32[128,64]{0,1:T(8,128)} %param.17) | copy-start | bytes 98308
  429.7 694.5 %all-reduce.3.cloned.1.call-start = ((), (), s32[]{:S(2)}) async-start(), calls=%async_computation.2 | async-start | bytes 131072 | tf_op jit(solution)/shard_map/psum | solution.py:111
  674.4 7.0 copy-start.2
Sparse Core Ops, SparseCore 0:
  122.6 78.9 all-gather.4
  429.9 70.8 all-gather.6
  686.3 437.8 all-reduce.2
